TPU v7x, 128 devices: a whole 4x4x4 slice. The times are simulated.
128 devices in a mesh: tok: 16 (over x, y), voc: 8 (over z, core).
Axes of the slice: x: 4, y: 4, z: 4, core: 2. Of those that a mesh axis runs over, the one named last changes fastest.
Arguments:
- hidden_rows: bfloat16 [512, 3584], P(('tok', 'voc')), may hold values from -40 to 40
- head_weight: bfloat16 [147456, 3584], P(('tok', 'voc')), may hold values from -0.09375 to 0.09375
- teacher_index: int32 [512, 64], replicated, may hold values from 0 to 147455, as said below
- teacher_logprob: float32 [512, 64], replicated, may hold values from -10 to -4.2
Outputs:
- row_loss: float32 [512], P(('tok', 'voc'))
- head_grad: bfloat16 [147456, 3584], P(('tok', 'voc'))
- input_grad: bfloat16 [512, 3584], P(('tok', 'voc'))
Inputs may be any that keep to these rules, and one draw needn't show every extreme that they name: `teacher_index`: the 64 entries of one token are distinct.
All inputs are finite; a program needn't handle non-finite values.
Results may differ from a plain program's by a relative error of at most 0.015.
Values may be sent and summed in bfloat16 or wider, within the bound.
No kernel may reach another device: no remote copies, remote signals or barrier semaphores. Data moves between devices by JAX's collectives and lax.ppermute only.
A program may use at most 128 MiB of HBM per device.

v0:
```python
import jax
import jax.numpy as jnp
from jax import lax
from jax.sharding import PartitionSpec as P

loss_scale = 256.0


def teacher_target(local, probs, voc_dev):
    blocks = local.shape[0] // 64
    local_b = local.reshape(blocks, 64, local.shape[1])
    probs_b = probs.reshape(blocks, 64, probs.shape[1])
    columns = jnp.arange(voc_dev, dtype=jnp.int32)[None, None, :]

    def one_block(args):
        block_local, block_probs = args
        equal = block_local[:, :, None] == columns
        return jnp.sum(jnp.where(equal, block_probs[:, :, None], 0.0), axis=1)

    return lax.map(one_block, (local_b, probs_b)).reshape(local.shape[0], voc_dev)


def per_device(hidden_rows, head_weight, teacher_index, teacher_logprob):
    voc_dev = head_weight.shape[0]
    tok_dev = hidden_rows.shape[0]
    every = lax.all_gather(hidden_rows, ("tok", "voc"), axis=0, tiled=True)
    logits = lax.dot_general(
        every, head_weight, (((1,), (1,)), ((), ())), preferred_element_type=jnp.float32
    )
    position = lax.axis_index(("tok", "voc"))
    offset = position * voc_dev
    local = teacher_index - offset
    probs = jnp.exp(teacher_logprob)
    target = teacher_target(local, probs, voc_dev)
    part_dot = jnp.sum(logits * target, axis=1)
    local_peak = jnp.max(logits, axis=1)
    peak = lax.pmax(local_peak, ("tok", "voc"))
    summed, dotted = lax.psum(
        (jnp.sum(jnp.exp(logits - peak[:, None]), axis=1), part_dot), ("tok", "voc")
    )
    lse = peak + jnp.log(summed)
    total_p = jnp.sum(probs, axis=1)
    own_term = jnp.sum(probs * teacher_logprob, axis=1)
    loss_all = own_term - dotted + total_p * lse
    row_loss = lax.dynamic_slice_in_dim(loss_all, position * tok_dev, tok_dev, 0)
    grad = (loss_scale * (total_p[:, None] * jnp.exp(logits - lse[:, None]) - target)).astype(
        jnp.bfloat16
    )
    head_grad = lax.dot_general(
        grad, every, (((0,), (0,)), ((), ())), preferred_element_type=jnp.float32
    ).astype(jnp.bfloat16)
    input_sum = lax.psum_scatter(
        jnp.dot(grad, head_weight, preferred_element_type=jnp.float32),
        ("tok", "voc"),
        scatter_dimension=0,
        tiled=True,
    )
    return (row_loss, head_grad, input_sum.astype(jnp.bfloat16))


def solution(mesh):
    placed = (P(("tok", "voc"), None), P(("tok", "voc"), None), P(), P())
    return jax.shard_map(
        per_device,
        mesh=mesh,
        in_specs=placed,
        out_specs=(P(("tok", "voc")), P(("tok", "voc"), None), P(("tok", "voc"), None)),
        check_vma=False,
    )
```

profile of v0, /device:TPU:0, one launch (start us, length us, event | category | flops | bytes accessed | tf_op | source)
XLA Modules:
  0.0 364.6 jit_solution(16396800213007242610)
XLA Ops:
  7.2 0.0 all-gather.3.cloned.1.call-start
  7.2 0.7 all-gather.3.cloned.1.call-update
  7.9 0.9 broadcast_subtract_fusion
  8.8 0.1 copy.11
  9.0 1.0 multiply_reduce_fusion
  9.9 0.1 copy.12
  10.1 28.0 %while.11 = (s32[]{:T(128)}, f32[8,64,1152]{2,1,0:T(8,128)S(1)}, s32[8,64,64]{2,1,0:T(8,128)S(1)}, f32[8,64,64]{2,1,0:T(8,128)S(1)}, s32[]{:T(128)}) while((s32[]{:T(128)}, f32[8,64,1152]{2,1,0:T(8,128)S(1)}, s32[8,64,64]{2,1,0:T(8,128)S(1)}, f32[8,64,64]{2,1,0:T(8,128)S(1)}, s32[]{:T(128)}) %tuple.35), condition=%wide.region_3.4_spmd.clone, body=%wide.region_1.3_spmd.clone.sunk | while | flops 14082050 | bytes 983113 | solution.py:20
  10.1 3.4 select_reduce_fusion.2
  13.6 3.4 select_reduce_fusion.2
  17.1 3.4 select_reduce_fusion.2
  20.6 3.4 select_reduce_fusion.2
  24.1 3.4 select_reduce_fusion.2
  27.6 3.4 select_reduce_fusion.2
  31.1 3.4 select_reduce_fusion.2
  34.6 3.4 select_reduce_fusion.2
  38.1 41.7 %all-gather.3.cloned.1.call-done = bf16[128,4,3584]{2,1,0:T(4,128)(2,1)} async-done(((bf16[1,4,3584]{2,1,0:T(4,128)(2,1)}), bf16[128,4,3584]{2,1,0:T(4,128)(2,1)}) %all-gather.3.cloned.1.call-update) | async-done | bytes 3670032 | tf_op jit(solution)/shard_map/all_gather | solution.py:26
  79.8 6.7 %reshape.26 = bf16[512,3584]{1,0:T(8,128)(2,1)} reshape(bf16[128,4,3584]{2,1,0:T(4,128)(2,1)} %all-gather.3.cloned.1.call-done) | data formatting | bytes 7340032
  86.5 10.9 %fusion.5 = (f32[512]{0:T(512)S(1)}, f32[512,1152]{1,0:T(8,128)}) fusion(bf16[512,3584]{1,0:T(8,128)(2,1)} %reshape.26, bf16[1152,3584]{1,0:T(8,128)(2,1)} %param.7), kind=kOutput, calls=%fused_computation.19 | convolution fusion | flops 4228447744 | bytes 14288896 | tf_op jit(solution)/shard_map/dot_general | solution.py:27
  97.4 62.7 %pmax.7 = f32[512]{0:T(512)S(1)} all-reduce(f32[512]{0:T(512)S(1)} %get-tuple-element.56), channel_id=1, replica_groups=mesh['tok'=16,'voc'=8] {'tok','voc'}, use_global_device_ids=true, to_apply=%region_8.9 | all-reduce | flops 512 | bytes 4096 | tf_op jit(solution)/shard_map/pmax | solution.py:37
  160.1 2.3 fusion.2
  162.4 64.3 %psum.15 = f32[512]{0:T(512)S(1)} all-reduce(f32[512]{0:T(512)S(1)} %get-tuple-element.42), channel_id=1, replica_groups=mesh['tok'=16,'voc'=8] {'tok','voc'}, use_global_device_ids=true, to_apply=%region_10.11 | all-reduce | flops 512 | bytes 4096 | tf_op jit(solution)/shard_map/psum | solution.py:38
  226.7 2.6 fusion.4
  229.3 0.0 copy-start
  229.3 10.4 %fusion.6 = f32[512,3584]{1,0:T(8,128)} fusion(bf16[512,1152]{1,0:T(8,128)(2,1)S(1)} %fusion.4, bf16[1152,3584]{1,0:T(8,128)(2,1)} %param.7), kind=kOutput, calls=%fused_computation.20 | convolution fusion | flops 4227858432 | bytes 16777216 | tf_op jit(solution)/shard_map/dot_general | solution.py:53
  239.7 0.0 copy-done
  239.7 6.7 %convolution_convert_fusion = bf16[1152,3584]{1,0:T(8,128)(2,1)} fusion(bf16[512,1152]{1,0:T(8,128)(2,1)S(1)} %fusion.4, bf16[512,3584]{1,0:T(8,128)(2,1)S(1)} %copy-done), kind=kOutput, calls=%fused_computation.6 | convolution fusion | flops 4231987200 | bytes 13107200 | tf_op jit(solution)/shard_map/dot_general | solution.py:49
  246.4 109.3 %all-reduce.3 = (f32[512]{0:T(512)S(1)}, bf16[512,3584]{1,0:T(8,128)(2,1)}) all-reduce(f32[512]{0:T(512)S(1)} %get-tuple-element.41, f32[512,3584]{1,0:T(8,128)} %fusion.6), channel_id=1, replica_groups=mesh['tok'=16,'voc'=8] {'tok','voc'}, use_global_device_ids=true, to_apply=%region_5.6 | all-reduce | flops 1835520 | bytes 11014144 | tf_op jit(solution)/shard_map/psum | solution.py:38
  355.7 0.6 dynamic_slice.11
  356.3 1.4 dynamic-slice_convert_fusion
  (27 shorter events, 0.4 us)
Async XLA Ops:
  7.2 72.6 %all-gather.3.cloned.1.call-start = ((), (), s32[]{:S(2)}) async-start(), calls=%async_computation | async-start | bytes 3698688 | tf_op jit(solution)/shard_map/all_gather | solution.py:26
  229.3 10.4 %copy-start = (bf16[512,3584]{1,0:T(8,128)(2,1)S(1)}, bf16[512,3584]{1,0:T(8,128)(2,1)}, u32[]{:S(2)}) copy-start(bf16[512,3584]{1,0:T(8,128)(2,1)} %reshape.26) | copy-start | bytes 11010052
Sparse Core Ops, SparseCore 0:
  11.0 68.7 all-gather.2
where the time goes:
time: 365 us
  blocking collectives  236 us (65%)
  waiting for transfers between devices  42.4 us (12%)
  other arithmetic  34 us (9%)
  matrix products  28 us (8%)
  between operations  14.1 us (4%)
  local copies, waits for them, and re-layouts  9.39 us (3%)
    psum x2, blocking collectives, per_device(): lax.psum((jnp.sum(jnp.exp(logits - peak[:, None]), axis=1), part_dot), ('...  174 us
    pmax x1, blocking collectives, per_device(): peak = lax.pmax(local_peak, ('tok', 'voc'))  62.7 us
    all_gather x1, waiting for transfers between devices, per_device(): every = lax.all_gather(hidden_rows, ('tok', 'voc'), axis=0, tiled=True)  41.7 us
    reduce_sum x8, other arithmetic, one_block(): return jnp.sum(jnp.where(equal, block_probs[:, :, None], 0.0), axis=1)  27.2 us
    dot_general x1, matrix products, per_device(): lax.dot_general(every, head_weight, (((1,), (1,)), ((), ())), preferred_e...  10.9 us
    dot_general x1, matrix products, per_device(): jnp.dot(grad, head_weight, preferred_element_type=jnp.float32)  10.4 us
  transfers between devices with their start and end apart: 1, of which 1 were waited for; matrix products, arithmetic and copies ran while one was open for 8% of the time, Pallas kernels for 0%

commit v1 on v0

--- a/solution.py
+++ b/solution.py
@@ -36,7 +36,7 @@
     local_peak = jnp.max(logits, axis=1)
     peak = lax.pmax(local_peak, ("tok", "voc"))
     summed, dotted = lax.psum(
-        (jnp.sum(jnp.exp(logits - peak[:, None]), axis=1), part_dot), ("tok", "voc")
+        lax.psum((jnp.sum(jnp.exp(logits - peak[:, None]), axis=1), part_dot), "tok"), "voc"
     )
     lse = peak + jnp.log(summed)
     total_p = jnp.sum(probs, axis=1)

time: 365 us -> 351 us (0.962)
  blocking collectives: 236 us -> 223 us
    psum x2, blocking collectives: 174 us -> 50.5 us  [the longest x1 38.1 us: per_device(): lax.psum((jnp.sum(jnp.exp(logits - peak[:, None]), axis=1), part_dot), 't...]
    unnamed x0 -> x1, blocking collectives: none -> 109 us
where the time goes in v1:
time: 351 us
  blocking collectives  223 us (64%)
  waiting for transfers between devices  42.4 us (12%)
  other arithmetic  34 us (10%)
  matrix products  28 us (8%)
  between operations  14.1 us (4%)
  local copies, waits for them, and re-layouts  9.38 us (3%)
    unnamed x1, blocking collectives  109 us
    pmax x1, blocking collectives, per_device(): peak = lax.pmax(local_peak, ('tok', 'voc'))  62.7 us
    all_gather x1, waiting for transfers between devices, per_device(): every = lax.all_gather(hidden_rows, ('tok', 'voc'), axis=0, tiled=True)  41.7 us
    psum x1, blocking collectives, per_device(): lax.psum((jnp.sum(jnp.exp(logits - peak[:, None]), axis=1), part_dot), 't...  38.1 us
    reduce_sum x8, other arithmetic, one_block(): return jnp.sum(jnp.where(equal, block_probs[:, :, None], 0.0), axis=1)  27.2 us
    psum x1, blocking collectives, per_device(): lax.psum(lax.psum((jnp.sum(jnp.exp(logits - peak[:, None]), axis=1), part...  12.4 us
    dot_general x1, matrix products, per_device(): lax.dot_general(every, head_weight, (((1,), (1,)), ((), ())), preferred_e...  10.9 us
    dot_general x1, matrix products, per_device(): jnp.dot(grad, head_weight, preferred_element_type=jnp.float32)  10.4 us
  transfers between devices with their start and end apart: 1, of which 1 were waited for; matrix products, arithmetic and copies ran while one was open for 8% of the time, Pallas kernels for 0%

profile of v1, /device:TPU:0, one launch (start us, length us, event | category | flops | bytes accessed | tf_op | source)
XLA Modules:
  0.0 350.9 jit_solution(14541141673544069546)
XLA Ops:
  7.2 0.0 all-gather.3.cloned.1.call-start
  7.2 0.7 all-gather.3.cloned.1.call-update
  7.9 0.9 broadcast_subtract_fusion
  8.8 0.1 copy.11
  9.0 1.0 multiply_reduce_fusion
  9.9 0.1 copy.12
  10.1 28.0 %while.11 = (s32[]{:T(128)}, f32[8,64,1152]{2,1,0:T(8,128)S(1)}, s32[8,64,64]{2,1,0:T(8,128)S(1)}, f32[8,64,64]{2,1,0:T(8,128)S(1)}, s32[]{:T(128)}) while((s32[]{:T(128)}, f32[8,64,1152]{2,1,0:T(8,128)S(1)}, s32[8,64,64]{2,1,0:T(8,128)S(1)}, f32[8,64,64]{2,1,0:T(8,128)S(1)}, s32[]{:T(128)}) %tuple.36), condition=%wide.region_3.4_spmd.clone, body=%wide.region_1.3_spmd.clone.sunk | while | flops 14082050 | bytes 983113 | solution.py:20
  10.1 3.4 select_reduce_fusion.2
  13.6 3.4 select_reduce_fusion.2
  17.1 3.4 select_reduce_fusion.2
  20.6 3.4 select_reduce_fusion.2
  24.1 3.4 select_reduce_fusion.2
  27.6 3.4 select_reduce_fusion.2
  31.1 3.4 select_reduce_fusion.2
  34.6 3.4 select_reduce_fusion.2
  38.1 41.7 %all-gather.3.cloned.1.call-done = bf16[128,4,3584]{2,1,0:T(4,128)(2,1)} async-done(((bf16[1,4,3584]{2,1,0:T(4,128)(2,1)}), bf16[128,4,3584]{2,1,0:T(4,128)(2,1)}) %all-gather.3.cloned.1.call-update) | async-done | bytes 3670032 | tf_op jit(solution)/shard_map/all_gather | solution.py:26
  79.8 6.7 %reshape.26 = bf16[512,3584]{1,0:T(8,128)(2,1)} reshape(bf16[128,4,3584]{2,1,0:T(4,128)(2,1)} %all-gather.3.cloned.1.call-done) | data formatting | bytes 7340032
  86.5 10.9 %fusion.5 = (f32[512]{0:T(512)S(1)}, f32[512,1152]{1,0:T(8,128)}) fusion(bf16[512,3584]{1,0:T(8,128)(2,1)} %reshape.26, bf16[1152,3584]{1,0:T(8,128)(2,1)} %param.7), kind=kOutput, calls=%fused_computation.19 | convolution fusion | flops 4228447744 | bytes 14288896 | tf_op jit(solution)/shard_map/dot_general | solution.py:27
  97.4 62.7 %pmax.7 = f32[512]{0:T(512)S(1)} all-reduce(f32[512]{0:T(512)S(1)} %get-tuple-element.60), channel_id=1, replica_groups=mesh['tok'=16,'voc'=8] {'tok','voc'}, use_global_device_ids=true, to_apply=%region_9.10 | all-reduce | flops 512 | bytes 4096 | tf_op jit(solution)/shard_map/pmax | solution.py:37
  160.1 2.3 fusion.2
  162.4 38.1 %all-reduce.1 = (f32[512]{0:T(512)S(1)}, f32[512]{0:T(512)S(1)}) all-reduce(f32[512]{0:T(512)S(1)} %get-tuple-element.42, f32[512]{0:T(512)S(1)} %get-tuple-element.41), channel_id=1, replica_groups=mesh['tok'=16,'voc'=8] {'tok'}, use_global_device_ids=true, to_apply=%region_11.12 | all-reduce | flops 1024 | bytes 8192 | tf_op jit(solution)/shard_map/psum | solution.py:39
  200.6 12.4 %all-reduce.2 = (f32[512]{0:T(512)S(1)}, f32[512]{0:T(512)S(1)}) all-reduce(f32[512]{0:T(512)S(1)} %get-tuple-element.53, f32[512]{0:T(512)S(1)} %get-tuple-element.54), channel_id=1, replica_groups=mesh['tok'=16,'voc'=8] {'voc'}, use_global_device_ids=true, to_apply=%region_12.13 | all-reduce | flops 1024 | bytes 8192 | tf_op jit(solution)/shard_map/psum | solution.py:38
  213.0 2.6 fusion.4
  215.6 0.0 copy-start
  215.6 10.4 %fusion.6 = f32[512,3584]{1,0:T(8,128)} fusion(bf16[512,1152]{1,0:T(8,128)(2,1)S(1)} %fusion.4, bf16[1152,3584]{1,0:T(8,128)(2,1)} %param.7), kind=kOutput, calls=%fused_computation.20 | convolution fusion | flops 4227858432 | bytes 16777216 | tf_op jit(solution)/shard_map/dot_general | solution.py:53
  226.0 0.0 copy-done
  226.0 6.7 %convolution_convert_fusion = bf16[1152,3584]{1,0:T(8,128)(2,1)} fusion(bf16[512,1152]{1,0:T(8,128)(2,1)S(1)} %fusion.4, bf16[512,3584]{1,0:T(8,128)(2,1)S(1)} %copy-done), kind=kOutput, calls=%fused_computation.6 | convolution fusion | flops 4231987200 | bytes 13107200 | tf_op jit(solution)/shard_map/dot_general | solution.py:49
  232.7 109.3 %all-reduce.4 = bf16[512,3584]{1,0:T(8,128)(2,1)} all-reduce(f32[512,3584]{1,0:T(8,128)} %fusion.6), channel_id=2, replica_groups=mesh['tok'=16,'voc'=8] {'tok','voc'}, use_global_device_ids=true, to_apply=%region_13.14.clone | all-reduce | flops 1835008 | bytes 11010048
  342.0 1.4 dynamic-slice_convert_fusion
  343.4 0.6 dynamic_slice.11
  (26 shorter events, 0.4 us)
Async XLA Ops:
  7.2 72.6 %all-gather.3.cloned.1.call-start = ((), (), s32[]{:S(2)}) async-start(), calls=%async_computation | async-start | bytes 3698688 | tf_op jit(solution)/shard_map/all_gather | solution.py:26
  215.6 10.4 %copy-start = (bf16[512,3584]{1,0:T(8,128)(2,1)S(1)}, bf16[512,3584]{1,0:T(8,128)(2,1)}, u32[]{:S(2)}) copy-start(bf16[512,3584]{1,0:T(8,128)(2,1)} %reshape.26) | copy-start | bytes 11010052
Sparse Core Ops, SparseCore 0:
  11.0 68.7 all-gather.2

commit v2 on v0

--- a/solution.py
+++ b/solution.py
@@ -23,7 +23,12 @@
 def per_device(hidden_rows, head_weight, teacher_index, teacher_logprob):
     voc_dev = head_weight.shape[0]
     tok_dev = hidden_rows.shape[0]
-    every = lax.all_gather(hidden_rows, ("tok", "voc"), axis=0, tiled=True)
+    every = jnp.concatenate(
+        lax.all_to_all(
+            jnp.stack([hidden_rows] * lax.axis_size(("tok", "voc"))), ("tok", "voc"), 0, 0
+        ),
+        axis=0,
+    )
     logits = lax.dot_general(
         every, head_weight, (((1,), (1,)), ((), ())), preferred_element_type=jnp.float32
     )

time: 365 us -> 341 us (0.934)
  waiting for transfers between devices: 42.4 us -> 18.8 us
  between operations: 14.1 us -> 0.73 us
  starting transfers between devices: 0.04 us -> 11.6 us
    all_gather x1 -> x0, waiting for transfers between devices: 41.7 us -> none  [per_device(): every = lax.all_gather(hidden_rows, ('tok', 'voc'), axis=0, tiled=True)]
    all_to_all x0 -> x1, waiting for transfers between devices: none -> 18.8 us  [per_device(): lax.all_to_all(jnp.stack([hidden_rows] * lax.axis_size(('tok', 'voc'))),...]
    all_to_all x0 -> x1, starting transfers between devices: none -> 11.6 us  [per_device(): lax.all_to_all(jnp.stack([hidden_rows] * lax.axis_size(('tok', 'voc'))),...]
    reshape x0 -> x1, local copies, waits for them, and re-layouts: none -> 6.73 us  [per_device(): jnp.concatenate(lax.all_to_all(jnp.stack([hidden_rows] * lax.axis_size(('...]
    unnamed x3 -> x6, local copies, waits for them, and re-layouts: 6.74 us -> 0.01 us
where the time goes in v2:
time: 341 us; the launch traced here: 340 us
  blocking collectives  235 us (69%)
  other arithmetic  32.2 us (9%)
  matrix products  28 us (8%)
  waiting for transfers between devices  18.8 us (6%)
  local copies, waits for them, and re-layouts  12.9 us (4%)
  starting transfers between devices  11.6 us (3%)
    psum x2, blocking collectives, per_device(): lax.psum((jnp.sum(jnp.exp(logits - peak[:, None]), axis=1), part_dot), ('...  173 us
    pmax x1, blocking collectives, per_device(): peak = lax.pmax(local_peak, ('tok', 'voc'))  62.5 us
    reduce_sum x8, other arithmetic, one_block(): return jnp.sum(jnp.where(equal, block_probs[:, :, None], 0.0), axis=1)  27.2 us
    all_to_all x1, waiting for transfers between devices, per_device(): lax.all_to_all(jnp.stack([hidden_rows] * lax.axis_size(('tok', 'voc'))),...  18.8 us
    all_to_all x1, starting transfers between devices, per_device(): lax.all_to_all(jnp.stack([hidden_rows] * lax.axis_size(('tok', 'voc'))),...  11.6 us
    dot_general x1, matrix products, per_device(): lax.dot_general(every, head_weight, (((1,), (1,)), ((), ())), preferred_e...  10.9 us
    dot_general x1, matrix products, per_device(): jnp.dot(grad, head_weight, preferred_element_type=jnp.float32)  10.4 us
  transfers between devices with their start and end apart: 1, of which 1 were waited for; matrix products, arithmetic and copies ran while one was open for 8% of the time, Pallas kernels for 0%

profile of v2, /device:TPU:0, one launch (start us, length us, event | category | flops | bytes accessed | tf_op | source)
XLA Modules:
  0.0 339.9 jit_solution(12822126608999091527)
XLA Ops:
  0.6 3.5 %stack.2 = bf16[128,4,3584]{2,1,0:T(4,128)(2,1)} broadcast(bf16[4,3584]{1,0:T(4,128)(2,1)} %param.6), dimensions={1,2} | broadcast | bytes 3698688 | tf_op jit(solution)/shard_map/stack | solution.py:28
  4.2 0.0 copy-start.1
  4.2 0.0 copy-start.2
  4.2 11.6 %all-to-all-start = ((bf16[128,4,3584]{2,1,0:T(4,128)(2,1)}), bf16[128,4,3584]{2,1,0:T(4,128)(2,1)}, u32[]{:S(2)}, u32[]{:S(2)}) async-start(bf16[128,4,3584]{2,1,0:T(4,128)(2,1)} %stack.2), calls=%async_computation | async-start | bytes 7340032 | tf_op jit(solution)/shard_map/all_to_all | solution.py:27
  15.8 0.0 copy-done.1
  15.8 0.1 copy.11
  16.0 0.0 copy-done.2
  16.0 0.1 copy.12
  16.1 28.0 %while.11 = (s32[]{:T(128)}, f32[8,64,1152]{2,1,0:T(8,128)S(1)}, s32[8,64,64]{2,1,0:T(8,128)S(1)}, f32[8,64,64]{2,1,0:T(8,128)S(1)}, s32[]{:T(128)}) while((s32[]{:T(128)}, f32[8,64,1152]{2,1,0:T(8,128)S(1)}, s32[8,64,64]{2,1,0:T(8,128)S(1)}, f32[8,64,64]{2,1,0:T(8,128)S(1)}, s32[]{:T(128)}) %tuple.33), condition=%wide.region_3.4_spmd.clone, body=%wide.region_1.3_spmd.clone.sunk | while | flops 14082050 | bytes 983113 | solution.py:20
  16.2 3.4 %select_reduce_fusion.2 = f32[64,1152]{1,0:T(8,128)S(1)} fusion(f32[64,64]{1,0:T(8,128)S(1)} %dynamic-slice_bitcast_fusion.4, s32[64,64]{1,0:T(8,128)S(1)} %dynamic-slice_bitcast_fusion.5), kind=kLoop, calls=%fused_computation.2.clone.1 | loop fusion | flops 14082048 | bytes 327680 | tf_op jit(solution)/shard_map/while/body/eval_jaxpr/reduce_sum | solution.py:18
  19.7 3.4 %select_reduce_fusion.2 = f32[64,1152]{1,0:T(8,128)S(1)} fusion(f32[64,64]{1,0:T(8,128)S(1)} %dynamic-slice_bitcast_fusion.4, s32[64,64]{1,0:T(8,128)S(1)} %dynamic-slice_bitcast_fusion.5), kind=kLoop, calls=%fused_computation.2.clone.1 | loop fusion | flops 14082048 | bytes 327680 | tf_op jit(solution)/shard_map/while/body/eval_jaxpr/reduce_sum | solution.py:18
  23.2 3.4 %select_reduce_fusion.2 = f32[64,1152]{1,0:T(8,128)S(1)} fusion(f32[64,64]{1,0:T(8,128)S(1)} %dynamic-slice_bitcast_fusion.4, s32[64,64]{1,0:T(8,128)S(1)} %dynamic-slice_bitcast_fusion.5), kind=kLoop, calls=%fused_computation.2.clone.1 | loop fusion | flops 14082048 | bytes 327680 | tf_op jit(solution)/shard_map/while/body/eval_jaxpr/reduce_sum | solution.py:18
  26.7 3.4 %select_reduce_fusion.2 = f32[64,1152]{1,0:T(8,128)S(1)} fusion(f32[64,64]{1,0:T(8,128)S(1)} %dynamic-slice_bitcast_fusion.4, s32[64,64]{1,0:T(8,128)S(1)} %dynamic-slice_bitcast_fusion.5), kind=kLoop, calls=%fused_computation.2.clone.1 | loop fusion | flops 14082048 | bytes 327680 | tf_op jit(solution)/shard_map/while/body/eval_jaxpr/reduce_sum | solution.py:18
  30.2 3.4 %select_reduce_fusion.2 = f32[64,1152]{1,0:T(8,128)S(1)} fusion(f32[64,64]{1,0:T(8,128)S(1)} %dynamic-slice_bitcast_fusion.4, s32[64,64]{1,0:T(8,128)S(1)} %dynamic-slice_bitcast_fusion.5), kind=kLoop, calls=%fused_computation.2.clone.1 | loop fusion | flops 14082048 | bytes 327680 | tf_op jit(solution)/shard_map/while/body/eval_jaxpr/reduce_sum | solution.py:18
  33.7 3.4 %select_reduce_fusion.2 = f32[64,1152]{1,0:T(8,128)S(1)} fusion(f32[64,64]{1,0:T(8,128)S(1)} %dynamic-slice_bitcast_fusion.4, s32[64,64]{1,0:T(8,128)S(1)} %dynamic-slice_bitcast_fusion.5), kind=kLoop, calls=%fused_computation.2.clone.1 | loop fusion | flops 14082048 | bytes 327680 | tf_op jit(solution)/shard_map/while/body/eval_jaxpr/reduce_sum | solution.py:18
  37.2 3.4 %select_reduce_fusion.2 = f32[64,1152]{1,0:T(8,128)S(1)} fusion(f32[64,64]{1,0:T(8,128)S(1)} %dynamic-slice_bitcast_fusion.4, s32[64,64]{1,0:T(8,128)S(1)} %dynamic-slice_bitcast_fusion.5), kind=kLoop, calls=%fused_computation.2.clone.1 | loop fusion | flops 14082048 | bytes 327680 | tf_op jit(solution)/shard_map/while/body/eval_jaxpr/reduce_sum | solution.py:18
  40.7 3.4 %select_reduce_fusion.2 = f32[64,1152]{1,0:T(8,128)S(1)} fusion(f32[64,64]{1,0:T(8,128)S(1)} %dynamic-slice_bitcast_fusion.4, s32[64,64]{1,0:T(8,128)S(1)} %dynamic-slice_bitcast_fusion.5), kind=kLoop, calls=%fused_computation.2.clone.1 | loop fusion | flops 14082048 | bytes 327680 | tf_op jit(solution)/shard_map/while/body/eval_jaxpr/reduce_sum | solution.py:18
  44.2 18.8 %all-to-all-done = bf16[128,4,3584]{2,1,0:T(4,128)(2,1)} async-done(((bf16[128,4,3584]{2,1,0:T(4,128)(2,1)}), bf16[128,4,3584]{2,1,0:T(4,128)(2,1)}, u32[]{:S(2)}, u32[]{:S(2)}) %all-to-all-start) | async-done | bytes 3670048 | tf_op jit(solution)/shard_map/all_to_all | solution.py:27
  62.9 6.7 %reshape.27 = bf16[512,3584]{1,0:T(8,128)(2,1)} reshape(bf16[128,4,3584]{2,1,0:T(4,128)(2,1)} %all-to-all-done) | data formatting | bytes 7340032 | tf_op jit(solution)/shard_map/reshape | solution.py:26
  69.6 10.9 %fusion.5 = (f32[512]{0:T(512)S(1)}, f32[512,1152]{1,0:T(8,128)}) fusion(bf16[512,3584]{1,0:T(8,128)(2,1)} %reshape.27, bf16[1152,3584]{1,0:T(8,128)(2,1)} %param.7), kind=kOutput, calls=%fused_computation.19 | convolution fusion | flops 4228447744 | bytes 14288896 | tf_op jit(solution)/shard_map/dot_general | solution.py:32
  80.5 62.5 %pmax.7 = f32[512]{0:T(512)S(1)} all-reduce(f32[512]{0:T(512)S(1)} %get-tuple-element.56), channel_id=1, replica_groups=mesh['tok'=16,'voc'=8] {'tok','voc'}, use_global_device_ids=true, to_apply=%region_8.9 | all-reduce | flops 512 | bytes 4096 | tf_op jit(solution)/shard_map/pmax | solution.py:42
  143.0 2.3 fusion.2
  145.3 62.7 %psum.15 = f32[512]{0:T(512)S(1)} all-reduce(f32[512]{0:T(512)S(1)} %get-tuple-element.42), channel_id=1, replica_groups=mesh['tok'=16,'voc'=8] {'tok','voc'}, use_global_device_ids=true, to_apply=%region_10.11 | all-reduce | flops 512 | bytes 4096 | tf_op jit(solution)/shard_map/psum | solution.py:43
  208.0 2.6 fusion.4
  210.5 0.0 copy-start
  210.5 10.4 %fusion.6 = f32[512,3584]{1,0:T(8,128)} fusion(bf16[512,1152]{1,0:T(8,128)(2,1)S(1)} %fusion.4, bf16[1152,3584]{1,0:T(8,128)(2,1)} %param.7), kind=kOutput, calls=%fused_computation.20 | convolution fusion | flops 4227858432 | bytes 16777216 | tf_op jit(solution)/shard_map/dot_general | solution.py:58
  221.0 0.0 copy-done
  221.0 6.7 %convolution_convert_fusion = bf16[1152,3584]{1,0:T(8,128)(2,1)} fusion(bf16[512,1152]{1,0:T(8,128)(2,1)S(1)} %fusion.4, bf16[512,3584]{1,0:T(8,128)(2,1)S(1)} %copy-done), kind=kOutput, calls=%fused_computation.6 | convolution fusion | flops 4231987200 | bytes 13107200 | tf_op jit(solution)/shard_map/dot_general | solution.py:54
  227.7 110.2 %all-reduce.3 = (f32[512]{0:T(512)S(1)}, bf16[512,3584]{1,0:T(8,128)(2,1)}) all-reduce(f32[512]{0:T(512)S(1)} %get-tuple-element.41, f32[512,3584]{1,0:T(8,128)} %fusion.6), channel_id=1, replica_groups=mesh['tok'=16,'voc'=8] {'tok','voc'}, use_global_device_ids=true, to_apply=%region_5.6 | all-reduce | flops 1835520 | bytes 11014144 | tf_op jit(solution)/shard_map/psum | solution.py:43
  337.8 0.6 dynamic_slice.11
  338.4 1.4 dynamic-slice_convert_fusion
  (29 shorter events, 0.5 us)
Async XLA Ops:
  4.2 11.6 %copy-start.1 = (s32[512,64]{0,1:T(8,128)S(1)}, s32[512,64]{0,1:T(8,128)}, u32[]{:S(2)}) copy-start(s32[512,64]{0,1:T(8,128)} %param.8) | copy-start | bytes 393220
  4.2 11.8 %copy-start.2 = (f32[512,64]{0,1:T(8,128)S(1)}, f32[512,64]{0,1:T(8,128)}, u32[]{:S(2)}) copy-start(f32[512,64]{0,1:T(8,128)} %param.9) | copy-start | bytes 393220
  4.2 58.7 %all-to-all-start = ((bf16[128,4,3584]{2,1,0:T(4,128)(2,1)}), bf16[128,4,3584]{2,1,0:T(4,128)(2,1)}, u32[]{:S(2)}, u32[]{:S(2)}) async-start(bf16[128,4,3584]{2,1,0:T(4,128)(2,1)} %stack.2), calls=%async_computation | async-start | bytes 7340032 | tf_op jit(solution)/shard_map/all_to_all | solution.py:27
  210.5 10.4 %copy-start = (bf16[512,3584]{1,0:T(8,128)(2,1)S(1)}, bf16[512,3584]{1,0:T(8,128)(2,1)}, u32[]{:S(2)}) copy-start(bf16[512,3584]{1,0:T(8,128)(2,1)} %reshape.27) | copy-start | bytes 11010052
